TPU v7x, 512 devices: a whole 4x8x8 slice. The times are simulated.
512 devices in a mesh: section: 32 (over z, x), neuron: 16 (over y, core).
Axes of the slice: x: 4, y: 8, z: 8, core: 2. Of those that a mesh axis runs over, the one named last changes fastest.
Arguments:
- inputs: bfloat16 [6, 32768], P(None, 'neuron'), may hold values from 0 to 2
- weight_tiles: bfloat16 [32, 2048, 128, 128], P('section', 'neuron'), may hold values from -0.07324219 to 0.07910156
- source_block: int32 [32, 2048], P('section', 'neuron'), may hold values from 0 to 255
- target_block: int32 [32, 2048], P('section', 'neuron'), may hold values from 0 to 15
- live_slots: int32 [32, 16], P('section', 'neuron'), may hold values from 16 to 128, as said below
Outputs:
- activations: bfloat16 [32, 6, 32768], P('section', None, 'neuron')
Inputs may be any that keep to these rules, and one draw needn't show every extreme that they name: live_slots[l, n] is 128, 64, 32 or 16, and in every layer some shard has all 128 slots live.
All inputs are finite; a program needn't handle non-finite values.
Results may differ from a plain program's by a relative error of at most 0.0045.
Values may be sent and summed in bfloat16 or wider, within the bound.
No kernel may reach another device: no remote copies, remote signals or barrier semaphores. Data moves between devices by JAX's collectives and lax.ppermute only.
A program may use at most 64 MiB of HBM per device.

v0:
```python
import jax
import jax.numpy as jnp
from jax import lax
from jax.sharding import PartitionSpec as P

MB = 3
NEURON_BIAS = -0.3
CLIP_LEVEL = 32.0


def from_behind(block, axis, distance):
    devices = range(lax.axis_size(axis))
    route = [(i - distance, i) for i in devices if i - distance in devices]
    return lax.ppermute(block, axis, route)


def layer_apply(gathered, weight_tiles, source_block, target_block, live_slots, column_count):
    row_count = gathered.shape[0]
    slot_count = weight_tiles.shape[1]
    block_size = weight_tiles.shape[2]
    block_count = gathered.shape[1] // block_size
    shaped = gathered.reshape(row_count, block_count, block_size)
    picked = jnp.take(shaped, source_block[0], axis=1)
    partial_value = jnp.einsum(
        "msk,skj->msj", picked, weight_tiles[0], preferred_element_type=jnp.float32
    )
    live_mask = jnp.arange(slot_count, dtype=jnp.int32) < live_slots[0, 0]
    selector = (
        target_block[0][:, None] == jnp.arange(column_count, dtype=jnp.int32)[None, :]
    ) & live_mask[:, None]
    summed = jnp.einsum(
        "msj,sc->mcj", partial_value, selector.astype(jnp.float32), precision=lax.Precision.HIGHEST
    )
    result = jnp.clip(summed + NEURON_BIAS, 0.0, CLIP_LEVEL).astype(jnp.bfloat16)
    return result.reshape(row_count, column_count * block_size)


def local(inputs, weight_tiles, source_block, target_block, live_slots):
    section_pos = lax.axis_index("section")
    section_count = lax.axis_size("section")
    total_rows = inputs.shape[0]
    shard_width = inputs.shape[1]
    column_count = shard_width // weight_tiles.shape[2]
    group_count = MB
    group_rows = total_rows // group_count
    step_count = section_count + group_count - 1

    def compute_layer(gathered):
        return layer_apply(
            gathered, weight_tiles, source_block, target_block, live_slots, column_count
        )

    def empty_layer(gathered):
        return jnp.zeros((group_rows, shard_width), jnp.bfloat16)

    def store_rows(collected, result, micro_index, active):
        row_start = jnp.clip(micro_index, 0, group_count - 1) * group_rows
        previous = lax.dynamic_slice_in_dim(collected, row_start, group_rows, 0)
        return lax.dynamic_update_slice_in_dim(
            collected, jnp.where(active, result, previous), row_start, 0
        )

    def input_rows(source, step_num):
        row_start = jnp.clip(step_num, 0, group_count - 1) * group_rows
        return lax.dynamic_slice_in_dim(source, row_start, group_rows, 0)

    collected = jnp.zeros((total_rows, shard_width), jnp.bfloat16)

    def advance(step_num, state_pair):
        current_in, collected = state_pair
        micro_index = step_num - section_pos
        active = (micro_index >= 0) & (micro_index < group_count)
        gathered = lax.all_gather(current_in, "neuron", axis=1, tiled=True)
        result = lax.cond(active, compute_layer, empty_layer, gathered)
        collected = store_rows(collected, result, micro_index, active)
        shifted = from_behind(result, "section", 1)
        current_in = jnp.where(section_pos == 0, input_rows(inputs, step_num + 1), shifted)
        return (current_in, collected)

    initial = input_rows(inputs, 0)
    final_in, collected = lax.fori_loop(0, step_count, advance, (initial, collected))
    return collected[None]


def solution(mesh):
    in_specs = (
        P(None, "neuron"),
        P("section", "neuron", None, None),
        P("section", "neuron"),
        P("section", "neuron"),
        P("section", "neuron"),
    )
    out_specs = P("section", None, "neuron")
    return jax.shard_map(local, mesh=mesh, in_specs=in_specs, out_specs=out_specs, check_vma=False)
```

profile of v0, /device:TPU:454, one launch (start us, length us, event | category | flops | bytes accessed | tf_op | source)
XLA Modules:
  0.0 940.5 jit_solution(12196027385270208893)
XLA Ops:
  0.8 939.1 %while.16 = (s32[]{:T(128)}, bf16[2,2048]{1,0:T(2,128)(2,1)S(1)}, bf16[6,2048]{1,0:T(8,128)(2,1)S(1)}, pred[]{:T(512)}, bf16[6,2048]{1,0:T(8,128)(2,1)}, /*index...) while((s32[]{:T(128)}, bf16[2,2048]{1,0:T(2,128)(2,1)S(1)}, ...), condition=%wide.region_3.0_spmd, body=%wide.region_0.3_spmd.sunk | while | flops 14739731 | bytes 4908993 | solution.py:81
  0.8 17.9 %all_gather.9 = bf16[2,32768]{1,0:T(2,128)(2,1)S(1)} all-gather(bf16[2,2048]{1,0:T(2,128)(2,1)S(1)} %get-tuple-element.321), channel_id=1, replica_groups=mesh['section'=32,'neuron'=16] {'neuron'}, dimensions={1}, use_global_device_ids=true | all-gather | bytes 139264 | tf_op jit(solution)/shard_map/while/body/eval_jaxpr/all_gather | solution.py:73
  25.1 15.3 %all_gather.9 = bf16[2,32768]{1,0:T(2,128)(2,1)S(1)} all-gather(bf16[2,2048]{1,0:T(2,128)(2,1)S(1)} %get-tuple-element.321), channel_id=1, replica_groups=mesh['section'=32,'neuron'=16] {'neuron'}, dimensions={1}, use_global_device_ids=true | all-gather | bytes 139264 | tf_op jit(solution)/shard_map/while/body/eval_jaxpr/all_gather | solution.py:73
  46.7 15.7 %all_gather.9 = bf16[2,32768]{1,0:T(2,128)(2,1)S(1)} all-gather(bf16[2,2048]{1,0:T(2,128)(2,1)S(1)} %get-tuple-element.321), channel_id=1, replica_groups=mesh['section'=32,'neuron'=16] {'neuron'}, dimensions={1}, use_global_device_ids=true | all-gather | bytes 139264 | tf_op jit(solution)/shard_map/while/body/eval_jaxpr/all_gather | solution.py:73
  68.7 15.3 %all_gather.9 = bf16[2,32768]{1,0:T(2,128)(2,1)S(1)} all-gather(bf16[2,2048]{1,0:T(2,128)(2,1)S(1)} %get-tuple-element.321), channel_id=1, replica_groups=mesh['section'=32,'neuron'=16] {'neuron'}, dimensions={1}, use_global_device_ids=true | all-gather | bytes 139264 | tf_op jit(solution)/shard_map/while/body/eval_jaxpr/all_gather | solution.py:73
  90.4 15.7 %all_gather.9 = bf16[2,32768]{1,0:T(2,128)(2,1)S(1)} all-gather(bf16[2,2048]{1,0:T(2,128)(2,1)S(1)} %get-tuple-element.321), channel_id=1, replica_groups=mesh['section'=32,'neuron'=16] {'neuron'}, dimensions={1}, use_global_device_ids=true | all-gather | bytes 139264 | tf_op jit(solution)/shard_map/while/body/eval_jaxpr/all_gather | solution.py:73
  112.5 15.3 %all_gather.9 = bf16[2,32768]{1,0:T(2,128)(2,1)S(1)} all-gather(bf16[2,2048]{1,0:T(2,128)(2,1)S(1)} %get-tuple-element.321), channel_id=1, replica_groups=mesh['section'=32,'neuron'=16] {'neuron'}, dimensions={1}, use_global_device_ids=true | all-gather | bytes 139264 | tf_op jit(solution)/shard_map/while/body/eval_jaxpr/all_gather | solution.py:73
  129.1 6.3 collective-permute-done
  136.2 15.7 %all_gather.9 = bf16[2,32768]{1,0:T(2,128)(2,1)S(1)} all-gather(bf16[2,2048]{1,0:T(2,128)(2,1)S(1)} %get-tuple-element.321), channel_id=1, replica_groups=mesh['section'=32,'neuron'=16] {'neuron'}, dimensions={1}, use_global_device_ids=true | all-gather | bytes 139264 | tf_op jit(solution)/shard_map/while/body/eval_jaxpr/all_gather | solution.py:73
  153.3 6.3 collective-permute-done
  160.4 15.3 %all_gather.9 = bf16[2,32768]{1,0:T(2,128)(2,1)S(1)} all-gather(bf16[2,2048]{1,0:T(2,128)(2,1)S(1)} %get-tuple-element.321), channel_id=1, replica_groups=mesh['section'=32,'neuron'=16] {'neuron'}, dimensions={1}, use_global_device_ids=true | all-gather | bytes 139264 | tf_op jit(solution)/shard_map/while/body/eval_jaxpr/all_gather | solution.py:73
  184.1 15.7 %all_gather.9 = bf16[2,32768]{1,0:T(2,128)(2,1)S(1)} all-gather(bf16[2,2048]{1,0:T(2,128)(2,1)S(1)} %get-tuple-element.321), channel_id=1, replica_groups=mesh['section'=32,'neuron'=16] {'neuron'}, dimensions={1}, use_global_device_ids=true | all-gather | bytes 139264 | tf_op jit(solution)/shard_map/while/body/eval_jaxpr/all_gather | solution.py:73
  201.1 6.3 collective-permute-done
  208.2 15.3 %all_gather.9 = bf16[2,32768]{1,0:T(2,128)(2,1)S(1)} all-gather(bf16[2,2048]{1,0:T(2,128)(2,1)S(1)} %get-tuple-element.321), channel_id=1, replica_groups=mesh['section'=32,'neuron'=16] {'neuron'}, dimensions={1}, use_global_device_ids=true | all-gather | bytes 139264 | tf_op jit(solution)/shard_map/while/body/eval_jaxpr/all_gather | solution.py:73
  224.9 6.3 collective-permute-done
  232.0 15.7 %all_gather.9 = bf16[2,32768]{1,0:T(2,128)(2,1)S(1)} all-gather(bf16[2,2048]{1,0:T(2,128)(2,1)S(1)} %get-tuple-element.321), channel_id=1, replica_groups=mesh['section'=32,'neuron'=16] {'neuron'}, dimensions={1}, use_global_device_ids=true | all-gather | bytes 139264 | tf_op jit(solution)/shard_map/while/body/eval_jaxpr/all_gather | solution.py:73
  256.1 15.3 %all_gather.9 = bf16[2,32768]{1,0:T(2,128)(2,1)S(1)} all-gather(bf16[2,2048]{1,0:T(2,128)(2,1)S(1)} %get-tuple-element.321), channel_id=1, replica_groups=mesh['section'=32,'neuron'=16] {'neuron'}, dimensions={1}, use_global_device_ids=true | all-gather | bytes 139264 | tf_op jit(solution)/shard_map/while/body/eval_jaxpr/all_gather | solution.py:73
  272.8 6.3 collective-permute-done
  279.9 15.7 %all_gather.9 = bf16[2,32768]{1,0:T(2,128)(2,1)S(1)} all-gather(bf16[2,2048]{1,0:T(2,128)(2,1)S(1)} %get-tuple-element.321), channel_id=1, replica_groups=mesh['section'=32,'neuron'=16] {'neuron'}, dimensions={1}, use_global_device_ids=true | all-gather | bytes 139264 | tf_op jit(solution)/shard_map/while/body/eval_jaxpr/all_gather | solution.py:73
  296.9 6.3 collective-permute-done
  304.0 15.3 %all_gather.9 = bf16[2,32768]{1,0:T(2,128)(2,1)S(1)} all-gather(bf16[2,2048]{1,0:T(2,128)(2,1)S(1)} %get-tuple-element.321), channel_id=1, replica_groups=mesh['section'=32,'neuron'=16] {'neuron'}, dimensions={1}, use_global_device_ids=true | all-gather | bytes 139264 | tf_op jit(solution)/shard_map/while/body/eval_jaxpr/all_gather | solution.py:73
  327.7 15.7 %all_gather.9 = bf16[2,32768]{1,0:T(2,128)(2,1)S(1)} all-gather(bf16[2,2048]{1,0:T(2,128)(2,1)S(1)} %get-tuple-element.321), channel_id=1, replica_groups=mesh['section'=32,'neuron'=16] {'neuron'}, dimensions={1}, use_global_device_ids=true | all-gather | bytes 139264 | tf_op jit(solution)/shard_map/while/body/eval_jaxpr/all_gather | solution.py:73
  344.8 6.3 collective-permute-done
  351.9 15.3 %all_gather.9 = bf16[2,32768]{1,0:T(2,128)(2,1)S(1)} all-gather(bf16[2,2048]{1,0:T(2,128)(2,1)S(1)} %get-tuple-element.321), channel_id=1, replica_groups=mesh['section'=32,'neuron'=16] {'neuron'}, dimensions={1}, use_global_device_ids=true | all-gather | bytes 139264 | tf_op jit(solution)/shard_map/while/body/eval_jaxpr/all_gather | solution.py:73
  375.6 15.7 %all_gather.9 = bf16[2,32768]{1,0:T(2,128)(2,1)S(1)} all-gather(bf16[2,2048]{1,0:T(2,128)(2,1)S(1)} %get-tuple-element.321), channel_id=1, replica_groups=mesh['section'=32,'neuron'=16] {'neuron'}, dimensions={1}, use_global_device_ids=true | all-gather | bytes 139264 | tf_op jit(solution)/shard_map/while/body/eval_jaxpr/all_gather | solution.py:73
  399.8 15.3 %all_gather.9 = bf16[2,32768]{1,0:T(2,128)(2,1)S(1)} all-gather(bf16[2,2048]{1,0:T(2,128)(2,1)S(1)} %get-tuple-element.321), channel_id=1, replica_groups=mesh['section'=32,'neuron'=16] {'neuron'}, dimensions={1}, use_global_device_ids=true | all-gather | bytes 139264 | tf_op jit(solution)/shard_map/while/body/eval_jaxpr/all_gather | solution.py:73
  423.5 15.7 %all_gather.9 = bf16[2,32768]{1,0:T(2,128)(2,1)S(1)} all-gather(bf16[2,2048]{1,0:T(2,128)(2,1)S(1)} %get-tuple-element.321), channel_id=1, replica_groups=mesh['section'=32,'neuron'=16] {'neuron'}, dimensions={1}, use_global_device_ids=true | all-gather | bytes 139264 | tf_op jit(solution)/shard_map/while/body/eval_jaxpr/all_gather | solution.py:73
  447.6 15.3 %all_gather.9 = bf16[2,32768]{1,0:T(2,128)(2,1)S(1)} all-gather(bf16[2,2048]{1,0:T(2,128)(2,1)S(1)} %get-tuple-element.321), channel_id=1, replica_groups=mesh['section'=32,'neuron'=16] {'neuron'}, dimensions={1}, use_global_device_ids=true | all-gather | bytes 139264 | tf_op jit(solution)/shard_map/while/body/eval_jaxpr/all_gather | solution.py:73
  471.4 15.7 %all_gather.9 = bf16[2,32768]{1,0:T(2,128)(2,1)S(1)} all-gather(bf16[2,2048]{1,0:T(2,128)(2,1)S(1)} %get-tuple-element.321), channel_id=1, replica_groups=mesh['section'=32,'neuron'=16] {'neuron'}, dimensions={1}, use_global_device_ids=true | all-gather | bytes 139264 | tf_op jit(solution)/shard_map/while/body/eval_jaxpr/all_gather | solution.py:73
  495.5 15.3 %all_gather.9 = bf16[2,32768]{1,0:T(2,128)(2,1)S(1)} all-gather(bf16[2,2048]{1,0:T(2,128)(2,1)S(1)} %get-tuple-element.321), channel_id=1, replica_groups=mesh['section'=32,'neuron'=16] {'neuron'}, dimensions={1}, use_global_device_ids=true | all-gather | bytes 139264 | tf_op jit(solution)/shard_map/while/body/eval_jaxpr/all_gather | solution.py:73
  519.3 15.7 %all_gather.9 = bf16[2,32768]{1,0:T(2,128)(2,1)S(1)} all-gather(bf16[2,2048]{1,0:T(2,128)(2,1)S(1)} %get-tuple-element.321), channel_id=1, replica_groups=mesh['section'=32,'neuron'=16] {'neuron'}, dimensions={1}, use_global_device_ids=true | all-gather | bytes 139264 | tf_op jit(solution)/shard_map/while/body/eval_jaxpr/all_gather | solution.py:73
  543.4 15.3 %all_gather.9 = bf16[2,32768]{1,0:T(2,128)(2,1)S(1)} all-gather(bf16[2,2048]{1,0:T(2,128)(2,1)S(1)} %get-tuple-element.321), channel_id=1, replica_groups=mesh['section'=32,'neuron'=16] {'neuron'}, dimensions={1}, use_global_device_ids=true | all-gather | bytes 139264 | tf_op jit(solution)/shard_map/while/body/eval_jaxpr/all_gather | solution.py:73
  567.1 15.7 %all_gather.9 = bf16[2,32768]{1,0:T(2,128)(2,1)S(1)} all-gather(bf16[2,2048]{1,0:T(2,128)(2,1)S(1)} %get-tuple-element.321), channel_id=1, replica_groups=mesh['section'=32,'neuron'=16] {'neuron'}, dimensions={1}, use_global_device_ids=true | all-gather | bytes 139264 | tf_op jit(solution)/shard_map/while/body/eval_jaxpr/all_gather | solution.py:73
  591.3 15.3 %all_gather.9 = bf16[2,32768]{1,0:T(2,128)(2,1)S(1)} all-gather(bf16[2,2048]{1,0:T(2,128)(2,1)S(1)} %get-tuple-element.321), channel_id=1, replica_groups=mesh['section'=32,'neuron'=16] {'neuron'}, dimensions={1}, use_global_device_ids=true | all-gather | bytes 139264 | tf_op jit(solution)/shard_map/while/body/eval_jaxpr/all_gather | solution.py:73
  615.0 15.7 %all_gather.9 = bf16[2,32768]{1,0:T(2,128)(2,1)S(1)} all-gather(bf16[2,2048]{1,0:T(2,128)(2,1)S(1)} %get-tuple-element.321), channel_id=1, replica_groups=mesh['section'=32,'neuron'=16] {'neuron'}, dimensions={1}, use_global_device_ids=true | all-gather | bytes 139264 | tf_op jit(solution)/shard_map/while/body/eval_jaxpr/all_gather | solution.py:73
  639.2 15.3 %all_gather.9 = bf16[2,32768]{1,0:T(2,128)(2,1)S(1)} all-gather(bf16[2,2048]{1,0:T(2,128)(2,1)S(1)} %get-tuple-element.321), channel_id=1, replica_groups=mesh['section'=32,'neuron'=16] {'neuron'}, dimensions={1}, use_global_device_ids=true | all-gather | bytes 139264 | tf_op jit(solution)/shard_map/while/body/eval_jaxpr/all_gather | solution.py:73
  662.9 15.7 %all_gather.9 = bf16[2,32768]{1,0:T(2,128)(2,1)S(1)} all-gather(bf16[2,2048]{1,0:T(2,128)(2,1)S(1)} %get-tuple-element.321), channel_id=1, replica_groups=mesh['section'=32,'neuron'=16] {'neuron'}, dimensions={1}, use_global_device_ids=true | all-gather | bytes 139264 | tf_op jit(solution)/shard_map/while/body/eval_jaxpr/all_gather | solution.py:73
  687.0 15.3 %all_gather.9 = bf16[2,32768]{1,0:T(2,128)(2,1)S(1)} all-gather(bf16[2,2048]{1,0:T(2,128)(2,1)S(1)} %get-tuple-element.321), channel_id=1, replica_groups=mesh['section'=32,'neuron'=16] {'neuron'}, dimensions={1}, use_global_device_ids=true | all-gather | bytes 139264 | tf_op jit(solution)/shard_map/while/body/eval_jaxpr/all_gather | solution.py:73
  710.8 15.7 %all_gather.9 = bf16[2,32768]{1,0:T(2,128)(2,1)S(1)} all-gather(bf16[2,2048]{1,0:T(2,128)(2,1)S(1)} %get-tuple-element.321), channel_id=1, replica_groups=mesh['section'=32,'neuron'=16] {'neuron'}, dimensions={1}, use_global_device_ids=true | all-gather | bytes 139264 | tf_op jit(solution)/shard_map/while/body/eval_jaxpr/all_gather | solution.py:73
  727.8 119.0 %collective-permute-done = bf16[2,2048]{1,0:T(2,128)(2,1)S(1)} collective-permute-done((bf16[2,2048]{1,0:T(2,128)(2,1)S(1)}, bf16[2,2048]{1,0:T(2,128)(2,1)S(1)}, u32[]{:S(2)}, u32[]{:S(2)}) %collective-permute-start) | collective-permute-done | bytes 8224 | tf_op jit(solution)/shard_map/while/body/eval_jaxpr/ppermute | solution.py:14
  847.6 16.5 %all_gather.9 = bf16[2,32768]{1,0:T(2,128)(2,1)S(1)} all-gather(bf16[2,2048]{1,0:T(2,128)(2,1)S(1)} %get-tuple-element.321), channel_id=1, replica_groups=mesh['section'=32,'neuron'=16] {'neuron'}, dimensions={1}, use_global_device_ids=true | all-gather | bytes 139264 | tf_op jit(solution)/shard_map/while/body/eval_jaxpr/all_gather | solution.py:73
  864.1 6.4 conditional.2
  871.8 7.5 collective-permute-done
  880.1 14.5 %all_gather.9 = bf16[2,32768]{1,0:T(2,128)(2,1)S(1)} all-gather(bf16[2,2048]{1,0:T(2,128)(2,1)S(1)} %get-tuple-element.321), channel_id=1, replica_groups=mesh['section'=32,'neuron'=16] {'neuron'}, dimensions={1}, use_global_device_ids=true | all-gather | bytes 139264 | tf_op jit(solution)/shard_map/while/body/eval_jaxpr/all_gather | solution.py:73
  894.7 6.4 conditional.2
  902.4 7.5 collective-permute-done
  910.7 16.5 %all_gather.9 = bf16[2,32768]{1,0:T(2,128)(2,1)S(1)} all-gather(bf16[2,2048]{1,0:T(2,128)(2,1)S(1)} %get-tuple-element.321), channel_id=1, replica_groups=mesh['section'=32,'neuron'=16] {'neuron'}, dimensions={1}, use_global_device_ids=true | all-gather | bytes 139264 | tf_op jit(solution)/shard_map/while/body/eval_jaxpr/all_gather | solution.py:73
  927.2 6.4 conditional.2
  (222 shorter events, 230.4 us)
Async XLA Ops:
  18.7 5.5 collective-permute-start
  40.4 5.5 collective-permute-start
  62.4 5.5 collective-permute-start
  84.0 5.5 collective-permute-start
  106.1 5.6 collective-permute-start
  127.8 7.6 collective-permute-start
  151.9 7.6 collective-permute-start
  175.6 7.6 collective-permute-start
  199.8 7.6 collective-permute-start
  223.5 7.6 collective-permute-start
  247.7 7.6 collective-permute-start
  271.4 7.6 collective-permute-start
  295.5 7.6 collective-permute-start
  319.3 7.6 collective-permute-start
  343.4 7.6 collective-permute-start
  367.2 7.6 collective-permute-start
  391.3 7.6 collective-permute-start
  415.0 7.6 collective-permute-start
  439.2 7.6 collective-permute-start
  462.9 7.6 collective-permute-start
  487.1 7.6 collective-permute-start
  510.8 7.6 collective-permute-start
  534.9 7.6 collective-permute-start
  558.7 7.6 collective-permute-start
  582.8 7.6 collective-permute-start
  606.6 7.6 collective-permute-start
  630.7 7.6 collective-permute-start
  654.4 7.6 collective-permute-start
  678.6 7.6 collective-permute-start
  702.3 7.6 collective-permute-start
  726.5 120.4 %collective-permute-start = (bf16[2,2048]{1,0:T(2,128)(2,1)S(1)}, bf16[2,2048]{1,0:T(2,128)(2,1)S(1)}, u32[]{:S(2)}, u32[]{:S(2)}) collective-permute-start(bf16[2,2048]{1,0:T(2,128)(2,1)S(1)} %get-tuple-element.350), channel_id=1, source_target_pairs={{0,16},{16,32},{32,48},{48,64},{64,80},{80,96},{96,112},{112,128},... | collective-permute-start | bytes 24584 | tf_op jit(solution)/shard_map/while/body/eval_jaxpr/ppermute | solution.py:14
  864.1 6.2 copy-start.1
  870.5 8.9 collective-permute-start
  894.7 6.2 copy-start.1
  901.0 8.9 collective-permute-start
  927.2 6.2 copy-start.1
  933.5 5.5 collective-permute-start
  939.9 0.6 copy-start
where the time goes:
time: 944 us; the launch traced here: 940 us
  blocking collectives  530 us (56%)
  waiting for transfers between devices  317 us (34%)
  starting transfers between devices  43.6 us (5%)
  other arithmetic  33.6 us (4%)
  matrix products  10.8 us (1%)
    all_gather x34, blocking collectives, advance(): gathered = lax.all_gather(current_in, 'neuron', axis=1, tiled=True)  530 us
    ppermute x34, waiting for transfers between devices, from_behind(): return lax.ppermute(block, axis, route)  317 us
    ppermute x34, starting transfers between devices, from_behind(): return lax.ppermute(block, axis, route)  43.6 us
    select_n x34, other arithmetic, advance(): jnp.where(section_pos == 0, input_rows(inputs, step_num + 1), shifted)  26.4 us
  transfers between devices with their start and end apart: 34, of which 34 were waited for; matrix products, arithmetic and copies ran while one was open for 0% of the time, Pallas kernels for 0%

commit v1 on v0

--- a/solution.py
+++ b/solution.py
@@ -70,7 +70,10 @@
         current_in, collected = state_pair
         micro_index = step_num - section_pos
         active = (micro_index >= 0) & (micro_index < group_count)
-        gathered = lax.all_gather(current_in, "neuron", axis=1, tiled=True)
+        devices_2 = lax.axis_size("neuron")
+        blocks = jnp.stack([current_in for _ in range(devices_2)])
+        blocks = lax.all_to_all(blocks, "neuron", split_axis=0, concat_axis=0)
+        gathered = jnp.concatenate(blocks, axis=1)
         result = lax.cond(active, compute_layer, empty_layer, gathered)
         collected = store_rows(collected, result, micro_index, active)
         shifted = from_behind(result, "section", 1)

time: 944 us -> 857 us (0.908)
  blocking collectives: 530 us -> 0 us
  waiting for transfers between devices: 317 us -> 609 us
  starting transfers between devices: 43.6 us -> 167 us
  local copies, waits for them, and re-layouts: 3.82 us -> 28.4 us
    all_gather x34 -> x0, blocking collectives: 530 us -> none  [advance(): gathered = lax.all_gather(current_in, 'neuron', axis=1, tiled=True)]
    all_to_all x0 -> x34, waiting for transfers between devices: none -> 292 us  [advance(): blocks = lax.all_to_all(blocks, 'neuron', split_axis=0, concat_axis=0)]
    all_to_all x0 -> x34, starting transfers between devices: none -> 123 us  [advance(): blocks = lax.all_to_all(blocks, 'neuron', split_axis=0, concat_axis=0)]
    another operation x31 -> x65, local copies, waits for them, and re-layouts: 0.21 us -> 24.8 us  [the longest x34 24.6 us: advance(): blocks = jnp.stack([current_in for _ in range(devices_2)])]
  transfers between devices with their start and end apart: 34 -> 68, of which waited for: 34 -> 68; matrix products, arithmetic and copies ran while one was open for 0% -> 0% of each run, Pallas kernels for 0% -> 0%
where the time goes in v1:
time: 857 us; the launch traced here: 851 us
  waiting for transfers between devices  609 us (71%)
  starting transfers between devices  167 us (19%)
  other arithmetic  33.6 us (4%)
  local copies, waits for them, and re-layouts  28.4 us (3%)
  matrix products  10.8 us (1%)
    ppermute x34, waiting for transfers between devices, from_behind(): return lax.ppermute(block, axis, route)  317 us
    all_to_all x34, waiting for transfers between devices, advance(): blocks = lax.all_to_all(blocks, 'neuron', split_axis=0, concat_axis=0)  292 us
    all_to_all x34, starting transfers between devices, advance(): blocks = lax.all_to_all(blocks, 'neuron', split_axis=0, concat_axis=0)  123 us
    ppermute x34, starting transfers between devices, from_behind(): return lax.ppermute(block, axis, route)  43.9 us
    select_n x34, other arithmetic, advance(): jnp.where(section_pos == 0, input_rows(inputs, step_num + 1), shifted)  26.4 us
    another operation x34, local copies, waits for them, and re-layouts, advance(): blocks = jnp.stack([current_in for _ in range(devices_2)])  24.6 us
  transfers between devices with their start and end apart: 68, of which 68 were waited for; matrix products, arithmetic and copies ran while one was open for 0% of the time, Pallas kernels for 0%

profile of v1, /device:TPU:454, one launch (start us, length us, event | category | flops | bytes accessed | tf_op | source)
XLA Modules:
  0.0 850.9 jit_solution(687123559328291019)
XLA Ops:
  0.8 849.5 %while.16 = (s32[]{:T(128)}, bf16[2,2048]{1,0:T(2,128)(2,1)S(1)}, bf16[6,2048]{1,0:T(8,128)(2,1)S(1)}, pred[]{:T(512)}, bf16[6,2048]{1,0:T(8,128)(2,1)}, /*index...) while((s32[]{:T(128)}, bf16[2,2048]{1,0:T(2,128)(2,1)S(1)}, ...), condition=%wide.region_3.0_spmd, body=%wide.region_0.3_spmd.sunk | while | flops 14739731 | bytes 5302241 | solution.py:84
  1.5 7.2 all-to-all-start
  8.8 8.6 %all-to-all-done = bf16[16,2,2048]{2,1,0:T(2,128)(2,1)S(1)} async-done(((bf16[16,2,2048]{2,1,0:T(2,128)(2,1)}), bf16[16,2,2048]{2,1,0:T(2,128)(2,1)S(1)}, u32[]{:S(2)}, u32[]{:S(2)}) %all-to-all-start) | async-done | bytes 131104 | tf_op jit(solution)/shard_map/while/body/eval_jaxpr/all_to_all | solution.py:75
  28.0 8.6 %all-to-all-done = bf16[16,2,2048]{2,1,0:T(2,128)(2,1)S(1)} async-done(((bf16[16,2,2048]{2,1,0:T(2,128)(2,1)}), bf16[16,2,2048]{2,1,0:T(2,128)(2,1)S(1)}, u32[]{:S(2)}, u32[]{:S(2)}) %all-to-all-start) | async-done | bytes 131104 | tf_op jit(solution)/shard_map/while/body/eval_jaxpr/all_to_all | solution.py:75
  47.2 8.6 %all-to-all-done = bf16[16,2,2048]{2,1,0:T(2,128)(2,1)S(1)} async-done(((bf16[16,2,2048]{2,1,0:T(2,128)(2,1)}), bf16[16,2,2048]{2,1,0:T(2,128)(2,1)S(1)}, u32[]{:S(2)}, u32[]{:S(2)}) %all-to-all-start) | async-done | bytes 131104 | tf_op jit(solution)/shard_map/while/body/eval_jaxpr/all_to_all | solution.py:75
  66.4 8.6 %all-to-all-done = bf16[16,2,2048]{2,1,0:T(2,128)(2,1)S(1)} async-done(((bf16[16,2,2048]{2,1,0:T(2,128)(2,1)}), bf16[16,2,2048]{2,1,0:T(2,128)(2,1)S(1)}, u32[]{:S(2)}, u32[]{:S(2)}) %all-to-all-start) | async-done | bytes 131104 | tf_op jit(solution)/shard_map/while/body/eval_jaxpr/all_to_all | solution.py:75
  85.6 8.6 %all-to-all-done = bf16[16,2,2048]{2,1,0:T(2,128)(2,1)S(1)} async-done(((bf16[16,2,2048]{2,1,0:T(2,128)(2,1)}), bf16[16,2,2048]{2,1,0:T(2,128)(2,1)S(1)}, u32[]{:S(2)}, u32[]{:S(2)}) %all-to-all-start) | async-done | bytes 131104 | tf_op jit(solution)/shard_map/while/body/eval_jaxpr/all_to_all | solution.py:75
  104.9 8.6 %all-to-all-done = bf16[16,2,2048]{2,1,0:T(2,128)(2,1)S(1)} async-done(((bf16[16,2,2048]{2,1,0:T(2,128)(2,1)}), bf16[16,2,2048]{2,1,0:T(2,128)(2,1)S(1)}, u32[]{:S(2)}, u32[]{:S(2)}) %all-to-all-start) | async-done | bytes 131104 | tf_op jit(solution)/shard_map/while/body/eval_jaxpr/all_to_all | solution.py:75
  126.2 8.6 %all-to-all-done = bf16[16,2,2048]{2,1,0:T(2,128)(2,1)S(1)} async-done(((bf16[16,2,2048]{2,1,0:T(2,128)(2,1)}), bf16[16,2,2048]{2,1,0:T(2,128)(2,1)S(1)}, u32[]{:S(2)}, u32[]{:S(2)}) %all-to-all-start) | async-done | bytes 131104 | tf_op jit(solution)/shard_map/while/body/eval_jaxpr/all_to_all | solution.py:75
  136.2 6.3 collective-permute-done
  147.5 8.6 %all-to-all-done = bf16[16,2,2048]{2,1,0:T(2,128)(2,1)S(1)} async-done(((bf16[16,2,2048]{2,1,0:T(2,128)(2,1)}), bf16[16,2,2048]{2,1,0:T(2,128)(2,1)S(1)}, u32[]{:S(2)}, u32[]{:S(2)}) %all-to-all-start) | async-done | bytes 131104 | tf_op jit(solution)/shard_map/while/body/eval_jaxpr/all_to_all | solution.py:75
  157.5 6.3 collective-permute-done
  168.9 8.6 %all-to-all-done = bf16[16,2,2048]{2,1,0:T(2,128)(2,1)S(1)} async-done(((bf16[16,2,2048]{2,1,0:T(2,128)(2,1)}), bf16[16,2,2048]{2,1,0:T(2,128)(2,1)S(1)}, u32[]{:S(2)}, u32[]{:S(2)}) %all-to-all-start) | async-done | bytes 131104 | tf_op jit(solution)/shard_map/while/body/eval_jaxpr/all_to_all | solution.py:75
  190.2 8.6 %all-to-all-done = bf16[16,2,2048]{2,1,0:T(2,128)(2,1)S(1)} async-done(((bf16[16,2,2048]{2,1,0:T(2,128)(2,1)}), bf16[16,2,2048]{2,1,0:T(2,128)(2,1)S(1)}, u32[]{:S(2)}, u32[]{:S(2)}) %all-to-all-start) | async-done | bytes 131104 | tf_op jit(solution)/shard_map/while/body/eval_jaxpr/all_to_all | solution.py:75
  200.1 6.3 collective-permute-done
  211.5 8.6 %all-to-all-done = bf16[16,2,2048]{2,1,0:T(2,128)(2,1)S(1)} async-done(((bf16[16,2,2048]{2,1,0:T(2,128)(2,1)}), bf16[16,2,2048]{2,1,0:T(2,128)(2,1)S(1)}, u32[]{:S(2)}, u32[]{:S(2)}) %all-to-all-start) | async-done | bytes 131104 | tf_op jit(solution)/shard_map/while/body/eval_jaxpr/all_to_all | solution.py:75
  221.4 6.3 collective-permute-done
  232.8 8.6 %all-to-all-done = bf16[16,2,2048]{2,1,0:T(2,128)(2,1)S(1)} async-done(((bf16[16,2,2048]{2,1,0:T(2,128)(2,1)}), bf16[16,2,2048]{2,1,0:T(2,128)(2,1)S(1)}, u32[]{:S(2)}, u32[]{:S(2)}) %all-to-all-start) | async-done | bytes 131104 | tf_op jit(solution)/shard_map/while/body/eval_jaxpr/all_to_all | solution.py:75
  254.1 8.6 %all-to-all-done = bf16[16,2,2048]{2,1,0:T(2,128)(2,1)S(1)} async-done(((bf16[16,2,2048]{2,1,0:T(2,128)(2,1)}), bf16[16,2,2048]{2,1,0:T(2,128)(2,1)S(1)}, u32[]{:S(2)}, u32[]{:S(2)}) %all-to-all-start) | async-done | bytes 131104 | tf_op jit(solution)/shard_map/while/body/eval_jaxpr/all_to_all | solution.py:75
  264.1 6.3 collective-permute-done
  275.5 8.6 %all-to-all-done = bf16[16,2,2048]{2,1,0:T(2,128)(2,1)S(1)} async-done(((bf16[16,2,2048]{2,1,0:T(2,128)(2,1)}), bf16[16,2,2048]{2,1,0:T(2,128)(2,1)S(1)}, u32[]{:S(2)}, u32[]{:S(2)}) %all-to-all-start) | async-done | bytes 131104 | tf_op jit(solution)/shard_map/while/body/eval_jaxpr/all_to_all | solution.py:75
  285.4 6.3 collective-permute-done
  296.8 8.6 %all-to-all-done = bf16[16,2,2048]{2,1,0:T(2,128)(2,1)S(1)} async-done(((bf16[16,2,2048]{2,1,0:T(2,128)(2,1)}), bf16[16,2,2048]{2,1,0:T(2,128)(2,1)S(1)}, u32[]{:S(2)}, u32[]{:S(2)}) %all-to-all-start) | async-done | bytes 131104 | tf_op jit(solution)/shard_map/while/body/eval_jaxpr/all_to_all | solution.py:75
  318.1 8.6 %all-to-all-done = bf16[16,2,2048]{2,1,0:T(2,128)(2,1)S(1)} async-done(((bf16[16,2,2048]{2,1,0:T(2,128)(2,1)}), bf16[16,2,2048]{2,1,0:T(2,128)(2,1)S(1)}, u32[]{:S(2)}, u32[]{:S(2)}) %all-to-all-start) | async-done | bytes 131104 | tf_op jit(solution)/shard_map/while/body/eval_jaxpr/all_to_all | solution.py:75
  339.4 8.6 %all-to-all-done = bf16[16,2,2048]{2,1,0:T(2,128)(2,1)S(1)} async-done(((bf16[16,2,2048]{2,1,0:T(2,128)(2,1)}), bf16[16,2,2048]{2,1,0:T(2,128)(2,1)S(1)}, u32[]{:S(2)}, u32[]{:S(2)}) %all-to-all-start) | async-done | bytes 131104 | tf_op jit(solution)/shard_map/while/body/eval_jaxpr/all_to_all | solution.py:75
  360.7 8.6 %all-to-all-done = bf16[16,2,2048]{2,1,0:T(2,128)(2,1)S(1)} async-done(((bf16[16,2,2048]{2,1,0:T(2,128)(2,1)}), bf16[16,2,2048]{2,1,0:T(2,128)(2,1)S(1)}, u32[]{:S(2)}, u32[]{:S(2)}) %all-to-all-start) | async-done | bytes 131104 | tf_op jit(solution)/shard_map/while/body/eval_jaxpr/all_to_all | solution.py:75
  382.1 8.6 %all-to-all-done = bf16[16,2,2048]{2,1,0:T(2,128)(2,1)S(1)} async-done(((bf16[16,2,2048]{2,1,0:T(2,128)(2,1)}), bf16[16,2,2048]{2,1,0:T(2,128)(2,1)S(1)}, u32[]{:S(2)}, u32[]{:S(2)}) %all-to-all-start) | async-done | bytes 131104 | tf_op jit(solution)/shard_map/while/body/eval_jaxpr/all_to_all | solution.py:75
  403.4 8.6 %all-to-all-done = bf16[16,2,2048]{2,1,0:T(2,128)(2,1)S(1)} async-done(((bf16[16,2,2048]{2,1,0:T(2,128)(2,1)}), bf16[16,2,2048]{2,1,0:T(2,128)(2,1)S(1)}, u32[]{:S(2)}, u32[]{:S(2)}) %all-to-all-start) | async-done | bytes 131104 | tf_op jit(solution)/shard_map/while/body/eval_jaxpr/all_to_all | solution.py:75
  424.7 8.6 %all-to-all-done = bf16[16,2,2048]{2,1,0:T(2,128)(2,1)S(1)} async-done(((bf16[16,2,2048]{2,1,0:T(2,128)(2,1)}), bf16[16,2,2048]{2,1,0:T(2,128)(2,1)S(1)}, u32[]{:S(2)}, u32[]{:S(2)}) %all-to-all-start) | async-done | bytes 131104 | tf_op jit(solution)/shard_map/while/body/eval_jaxpr/all_to_all | solution.py:75
  446.0 8.6 %all-to-all-done = bf16[16,2,2048]{2,1,0:T(2,128)(2,1)S(1)} async-done(((bf16[16,2,2048]{2,1,0:T(2,128)(2,1)}), bf16[16,2,2048]{2,1,0:T(2,128)(2,1)S(1)}, u32[]{:S(2)}, u32[]{:S(2)}) %all-to-all-start) | async-done | bytes 131104 | tf_op jit(solution)/shard_map/while/body/eval_jaxpr/all_to_all | solution.py:75
  467.3 8.6 %all-to-all-done = bf16[16,2,2048]{2,1,0:T(2,128)(2,1)S(1)} async-done(((bf16[16,2,2048]{2,1,0:T(2,128)(2,1)}), bf16[16,2,2048]{2,1,0:T(2,128)(2,1)S(1)}, u32[]{:S(2)}, u32[]{:S(2)}) %all-to-all-start) | async-done | bytes 131104 | tf_op jit(solution)/shard_map/while/body/eval_jaxpr/all_to_all | solution.py:75
  488.6 8.6 %all-to-all-done = bf16[16,2,2048]{2,1,0:T(2,128)(2,1)S(1)} async-done(((bf16[16,2,2048]{2,1,0:T(2,128)(2,1)}), bf16[16,2,2048]{2,1,0:T(2,128)(2,1)S(1)}, u32[]{:S(2)}, u32[]{:S(2)}) %all-to-all-start) | async-done | bytes 131104 | tf_op jit(solution)/shard_map/while/body/eval_jaxpr/all_to_all | solution.py:75
  510.0 8.6 %all-to-all-done = bf16[16,2,2048]{2,1,0:T(2,128)(2,1)S(1)} async-done(((bf16[16,2,2048]{2,1,0:T(2,128)(2,1)}), bf16[16,2,2048]{2,1,0:T(2,128)(2,1)S(1)}, u32[]{:S(2)}, u32[]{:S(2)}) %all-to-all-start) | async-done | bytes 131104 | tf_op jit(solution)/shard_map/while/body/eval_jaxpr/all_to_all | solution.py:75
  531.3 8.6 %all-to-all-done = bf16[16,2,2048]{2,1,0:T(2,128)(2,1)S(1)} async-done(((bf16[16,2,2048]{2,1,0:T(2,128)(2,1)}), bf16[16,2,2048]{2,1,0:T(2,128)(2,1)S(1)}, u32[]{:S(2)}, u32[]{:S(2)}) %all-to-all-start) | async-done | bytes 131104 | tf_op jit(solution)/shard_map/while/body/eval_jaxpr/all_to_all | solution.py:75
  552.6 8.6 %all-to-all-done = bf16[16,2,2048]{2,1,0:T(2,128)(2,1)S(1)} async-done(((bf16[16,2,2048]{2,1,0:T(2,128)(2,1)}), bf16[16,2,2048]{2,1,0:T(2,128)(2,1)S(1)}, u32[]{:S(2)}, u32[]{:S(2)}) %all-to-all-start) | async-done | bytes 131104 | tf_op jit(solution)/shard_map/while/body/eval_jaxpr/all_to_all | solution.py:75
  573.9 8.6 %all-to-all-done = bf16[16,2,2048]{2,1,0:T(2,128)(2,1)S(1)} async-done(((bf16[16,2,2048]{2,1,0:T(2,128)(2,1)}), bf16[16,2,2048]{2,1,0:T(2,128)(2,1)S(1)}, u32[]{:S(2)}, u32[]{:S(2)}) %all-to-all-start) | async-done | bytes 131104 | tf_op jit(solution)/shard_map/while/body/eval_jaxpr/all_to_all | solution.py:75
  595.2 8.6 %all-to-all-done = bf16[16,2,2048]{2,1,0:T(2,128)(2,1)S(1)} async-done(((bf16[16,2,2048]{2,1,0:T(2,128)(2,1)}), bf16[16,2,2048]{2,1,0:T(2,128)(2,1)S(1)}, u32[]{:S(2)}, u32[]{:S(2)}) %all-to-all-start) | async-done | bytes 131104 | tf_op jit(solution)/shard_map/while/body/eval_jaxpr/all_to_all | solution.py:75
  616.6 8.6 %all-to-all-done = bf16[16,2,2048]{2,1,0:T(2,128)(2,1)S(1)} async-done(((bf16[16,2,2048]{2,1,0:T(2,128)(2,1)}), bf16[16,2,2048]{2,1,0:T(2,128)(2,1)S(1)}, u32[]{:S(2)}, u32[]{:S(2)}) %all-to-all-start) | async-done | bytes 131104 | tf_op jit(solution)/shard_map/while/body/eval_jaxpr/all_to_all | solution.py:75
  637.9 8.6 %all-to-all-done = bf16[16,2,2048]{2,1,0:T(2,128)(2,1)S(1)} async-done(((bf16[16,2,2048]{2,1,0:T(2,128)(2,1)}), bf16[16,2,2048]{2,1,0:T(2,128)(2,1)S(1)}, u32[]{:S(2)}, u32[]{:S(2)}) %all-to-all-start) | async-done | bytes 131104 | tf_op jit(solution)/shard_map/while/body/eval_jaxpr/all_to_all | solution.py:75
  647.8 118.3 %collective-permute-done = bf16[2,2048]{1,0:T(2,128)(2,1)S(1)} collective-permute-done((bf16[2,2048]{1,0:T(2,128)(2,1)S(1)}, bf16[2,2048]{1,0:T(2,128)(2,1)S(1)}, u32[]{:S(2)}, u32[]{:S(2)}) %collective-permute-start) | collective-permute-done | bytes 8224 | tf_op jit(solution)/shard_map/while/body/eval_jaxpr/ppermute | solution.py:14
  771.2 8.6 %all-to-all-done = bf16[16,2,2048]{2,1,0:T(2,128)(2,1)S(1)} async-done(((bf16[16,2,2048]{2,1,0:T(2,128)(2,1)}), bf16[16,2,2048]{2,1,0:T(2,128)(2,1)S(1)}, u32[]{:S(2)}, u32[]{:S(2)}) %all-to-all-start) | async-done | bytes 131104 | tf_op jit(solution)/shard_map/while/body/eval_jaxpr/all_to_all | solution.py:75
  779.8 6.4 conditional.2
  787.5 7.5 collective-permute-done
  800.1 8.6 %all-to-all-done = bf16[16,2,2048]{2,1,0:T(2,128)(2,1)S(1)} async-done(((bf16[16,2,2048]{2,1,0:T(2,128)(2,1)}), bf16[16,2,2048]{2,1,0:T(2,128)(2,1)S(1)}, u32[]{:S(2)}, u32[]{:S(2)}) %all-to-all-start) | async-done | bytes 131104 | tf_op jit(solution)/shard_map/while/body/eval_jaxpr/all_to_all | solution.py:75
  808.7 6.4 conditional.2
  816.4 7.5 collective-permute-done
  829.0 8.6 %all-to-all-done = bf16[16,2,2048]{2,1,0:T(2,128)(2,1)S(1)} async-done(((bf16[16,2,2048]{2,1,0:T(2,128)(2,1)}), bf16[16,2,2048]{2,1,0:T(2,128)(2,1)S(1)}, u32[]{:S(2)}, u32[]{:S(2)}) %all-to-all-start) | async-done | bytes 131104 | tf_op jit(solution)/shard_map/while/body/eval_jaxpr/all_to_all | solution.py:75
  837.6 6.4 conditional.2
  (290 shorter events, 378.1 us)
Async XLA Ops:
  1.5 15.9 %all-to-all-start = ((bf16[16,2,2048]{2,1,0:T(2,128)(2,1)}), bf16[16,2,2048]{2,1,0:T(2,128)(2,1)S(1)}, u32[]{:S(2)}, u32[]{:S(2)}) async-start(bf16[16,2,2048]{2,1,0:T(2,128)(2,1)} %stack.7), calls=%async_computation | async-start | bytes 262144 | tf_op jit(solution)/shard_map/while/body/eval_jaxpr/all_to_all | solution.py:75
  24.4 12.1 %all-to-all-start = ((bf16[16,2,2048]{2,1,0:T(2,128)(2,1)}), bf16[16,2,2048]{2,1,0:T(2,128)(2,1)S(1)}, u32[]{:S(2)}, u32[]{:S(2)}) async-start(bf16[16,2,2048]{2,1,0:T(2,128)(2,1)} %stack.7), calls=%async_computation | async-start | bytes 262144 | tf_op jit(solution)/shard_map/while/body/eval_jaxpr/all_to_all | solution.py:75
  43.7 12.1 %all-to-all-start = ((bf16[16,2,2048]{2,1,0:T(2,128)(2,1)}), bf16[16,2,2048]{2,1,0:T(2,128)(2,1)S(1)}, u32[]{:S(2)}, u32[]{:S(2)}) async-start(bf16[16,2,2048]{2,1,0:T(2,128)(2,1)} %stack.7), calls=%async_computation | async-start | bytes 262144 | tf_op jit(solution)/shard_map/while/body/eval_jaxpr/all_to_all | solution.py:75
  62.9 12.1 %all-to-all-start = ((bf16[16,2,2048]{2,1,0:T(2,128)(2,1)}), bf16[16,2,2048]{2,1,0:T(2,128)(2,1)S(1)}, u32[]{:S(2)}, u32[]{:S(2)}) async-start(bf16[16,2,2048]{2,1,0:T(2,128)(2,1)} %stack.7), calls=%async_computation | async-start | bytes 262144 | tf_op jit(solution)/shard_map/while/body/eval_jaxpr/all_to_all | solution.py:75
  82.1 12.1 %all-to-all-start = ((bf16[16,2,2048]{2,1,0:T(2,128)(2,1)}), bf16[16,2,2048]{2,1,0:T(2,128)(2,1)S(1)}, u32[]{:S(2)}, u32[]{:S(2)}) async-start(bf16[16,2,2048]{2,1,0:T(2,128)(2,1)} %stack.7), calls=%async_computation | async-start | bytes 262144 | tf_op jit(solution)/shard_map/while/body/eval_jaxpr/all_to_all | solution.py:75
  101.4 12.1 %all-to-all-start = ((bf16[16,2,2048]{2,1,0:T(2,128)(2,1)}), bf16[16,2,2048]{2,1,0:T(2,128)(2,1)S(1)}, u32[]{:S(2)}, u32[]{:S(2)}) async-start(bf16[16,2,2048]{2,1,0:T(2,128)(2,1)} %stack.7), calls=%async_computation | async-start | bytes 262144 | tf_op jit(solution)/shard_map/while/body/eval_jaxpr/all_to_all | solution.py:75
  122.7 12.1 %all-to-all-start = ((bf16[16,2,2048]{2,1,0:T(2,128)(2,1)}), bf16[16,2,2048]{2,1,0:T(2,128)(2,1)S(1)}, u32[]{:S(2)}, u32[]{:S(2)}) async-start(bf16[16,2,2048]{2,1,0:T(2,128)(2,1)} %stack.7), calls=%async_computation | async-start | bytes 262144 | tf_op jit(solution)/shard_map/while/body/eval_jaxpr/all_to_all | solution.py:75
  134.8 7.7 collective-permute-start
  144.0 12.1 %all-to-all-start = ((bf16[16,2,2048]{2,1,0:T(2,128)(2,1)}), bf16[16,2,2048]{2,1,0:T(2,128)(2,1)S(1)}, u32[]{:S(2)}, u32[]{:S(2)}) async-start(bf16[16,2,2048]{2,1,0:T(2,128)(2,1)} %stack.7), calls=%async_computation | async-start | bytes 262144 | tf_op jit(solution)/shard_map/while/body/eval_jaxpr/all_to_all | solution.py:75
  156.1 7.7 collective-permute-start
  165.3 12.1 %all-to-all-start = ((bf16[16,2,2048]{2,1,0:T(2,128)(2,1)}), bf16[16,2,2048]{2,1,0:T(2,128)(2,1)S(1)}, u32[]{:S(2)}, u32[]{:S(2)}) async-start(bf16[16,2,2048]{2,1,0:T(2,128)(2,1)} %stack.7), calls=%async_computation | async-start | bytes 262144 | tf_op jit(solution)/shard_map/while/body/eval_jaxpr/all_to_all | solution.py:75
  186.6 12.1 %all-to-all-start = ((bf16[16,2,2048]{2,1,0:T(2,128)(2,1)}), bf16[16,2,2048]{2,1,0:T(2,128)(2,1)S(1)}, u32[]{:S(2)}, u32[]{:S(2)}) async-start(bf16[16,2,2048]{2,1,0:T(2,128)(2,1)} %stack.7), calls=%async_computation | async-start | bytes 262144 | tf_op jit(solution)/shard_map/while/body/eval_jaxpr/all_to_all | solution.py:75
  198.8 7.7 collective-permute-start
  208.0 12.1 %all-to-all-start = ((bf16[16,2,2048]{2,1,0:T(2,128)(2,1)}), bf16[16,2,2048]{2,1,0:T(2,128)(2,1)S(1)}, u32[]{:S(2)}, u32[]{:S(2)}) async-start(bf16[16,2,2048]{2,1,0:T(2,128)(2,1)} %stack.7), calls=%async_computation | async-start | bytes 262144 | tf_op jit(solution)/shard_map/while/body/eval_jaxpr/all_to_all | solution.py:75
  229.3 12.1 %all-to-all-start = ((bf16[16,2,2048]{2,1,0:T(2,128)(2,1)}), bf16[16,2,2048]{2,1,0:T(2,128)(2,1)S(1)}, u32[]{:S(2)}, u32[]{:S(2)}) async-start(bf16[16,2,2048]{2,1,0:T(2,128)(2,1)} %stack.7), calls=%async_computation | async-start | bytes 262144 | tf_op jit(solution)/shard_map/while/body/eval_jaxpr/all_to_all | solution.py:75
  250.6 12.1 %all-to-all-start = ((bf16[16,2,2048]{2,1,0:T(2,128)(2,1)}), bf16[16,2,2048]{2,1,0:T(2,128)(2,1)S(1)}, u32[]{:S(2)}, u32[]{:S(2)}) async-start(bf16[16,2,2048]{2,1,0:T(2,128)(2,1)} %stack.7), calls=%async_computation | async-start | bytes 262144 | tf_op jit(solution)/shard_map/while/body/eval_jaxpr/all_to_all | solution.py:75
  262.7 7.7 collective-permute-start
  271.9 12.1 %all-to-all-start = ((bf16[16,2,2048]{2,1,0:T(2,128)(2,1)}), bf16[16,2,2048]{2,1,0:T(2,128)(2,1)S(1)}, u32[]{:S(2)}, u32[]{:S(2)}) async-start(bf16[16,2,2048]{2,1,0:T(2,128)(2,1)} %stack.7), calls=%async_computation | async-start | bytes 262144 | tf_op jit(solution)/shard_map/while/body/eval_jaxpr/all_to_all | solution.py:75
  293.2 12.1 %all-to-all-start = ((bf16[16,2,2048]{2,1,0:T(2,128)(2,1)}), bf16[16,2,2048]{2,1,0:T(2,128)(2,1)S(1)}, u32[]{:S(2)}, u32[]{:S(2)}) async-start(bf16[16,2,2048]{2,1,0:T(2,128)(2,1)} %stack.7), calls=%async_computation | async-start | bytes 262144 | tf_op jit(solution)/shard_map/while/body/eval_jaxpr/all_to_all | solution.py:75
  305.4 7.7 collective-permute-start
  314.5 12.1 %all-to-all-start = ((bf16[16,2,2048]{2,1,0:T(2,128)(2,1)}), bf16[16,2,2048]{2,1,0:T(2,128)(2,1)S(1)}, u32[]{:S(2)}, u32[]{:S(2)}) async-start(bf16[16,2,2048]{2,1,0:T(2,128)(2,1)} %stack.7), calls=%async_computation | async-start | bytes 262144 | tf_op jit(solution)/shard_map/while/body/eval_jaxpr/all_to_all | solution.py:75
  326.7 7.7 collective-permute-start
  335.9 12.1 %all-to-all-start = ((bf16[16,2,2048]{2,1,0:T(2,128)(2,1)}), bf16[16,2,2048]{2,1,0:T(2,128)(2,1)S(1)}, u32[]{:S(2)}, u32[]{:S(2)}) async-start(bf16[16,2,2048]{2,1,0:T(2,128)(2,1)} %stack.7), calls=%async_computation | async-start | bytes 262144 | tf_op jit(solution)/shard_map/while/body/eval_jaxpr/all_to_all | solution.py:75
  357.2 12.1 %all-to-all-start = ((bf16[16,2,2048]{2,1,0:T(2,128)(2,1)}), bf16[16,2,2048]{2,1,0:T(2,128)(2,1)S(1)}, u32[]{:S(2)}, u32[]{:S(2)}) async-start(bf16[16,2,2048]{2,1,0:T(2,128)(2,1)} %stack.7), calls=%async_computation | async-start | bytes 262144 | tf_op jit(solution)/shard_map/while/body/eval_jaxpr/all_to_all | solution.py:75
  369.3 7.7 collective-permute-start
  378.5 12.1 %all-to-all-start = ((bf16[16,2,2048]{2,1,0:T(2,128)(2,1)}), bf16[16,2,2048]{2,1,0:T(2,128)(2,1)S(1)}, u32[]{:S(2)}, u32[]{:S(2)}) async-start(bf16[16,2,2048]{2,1,0:T(2,128)(2,1)} %stack.7), calls=%async_computation | async-start | bytes 262144 | tf_op jit(solution)/shard_map/while/body/eval_jaxpr/all_to_all | solution.py:75
  399.8 12.1 %all-to-all-start = ((bf16[16,2,2048]{2,1,0:T(2,128)(2,1)}), bf16[16,2,2048]{2,1,0:T(2,128)(2,1)S(1)}, u32[]{:S(2)}, u32[]{:S(2)}) async-start(bf16[16,2,2048]{2,1,0:T(2,128)(2,1)} %stack.7), calls=%async_computation | async-start | bytes 262144 | tf_op jit(solution)/shard_map/while/body/eval_jaxpr/all_to_all | solution.py:75
  421.1 12.1 %all-to-all-start = ((bf16[16,2,2048]{2,1,0:T(2,128)(2,1)}), bf16[16,2,2048]{2,1,0:T(2,128)(2,1)S(1)}, u32[]{:S(2)}, u32[]{:S(2)}) async-start(bf16[16,2,2048]{2,1,0:T(2,128)(2,1)} %stack.7), calls=%async_computation | async-start | bytes 262144 | tf_op jit(solution)/shard_map/while/body/eval_jaxpr/all_to_all | solution.py:75
  433.3 7.7 collective-permute-start
  442.5 12.1 %all-to-all-start = ((bf16[16,2,2048]{2,1,0:T(2,128)(2,1)}), bf16[16,2,2048]{2,1,0:T(2,128)(2,1)S(1)}, u32[]{:S(2)}, u32[]{:S(2)}) async-start(bf16[16,2,2048]{2,1,0:T(2,128)(2,1)} %stack.7), calls=%async_computation | async-start | bytes 262144 | tf_op jit(solution)/shard_map/while/body/eval_jaxpr/all_to_all | solution.py:75
  463.8 12.1 %all-to-all-start = ((bf16[16,2,2048]{2,1,0:T(2,128)(2,1)}), bf16[16,2,2048]{2,1,0:T(2,128)(2,1)S(1)}, u32[]{:S(2)}, u32[]{:S(2)}) async-start(bf16[16,2,2048]{2,1,0:T(2,128)(2,1)} %stack.7), calls=%async_computation | async-start | bytes 262144 | tf_op jit(solution)/shard_map/while/body/eval_jaxpr/all_to_all | solution.py:75
  475.9 7.7 collective-permute-start
  485.1 12.1 %all-to-all-start = ((bf16[16,2,2048]{2,1,0:T(2,128)(2,1)}), bf16[16,2,2048]{2,1,0:T(2,128)(2,1)S(1)}, u32[]{:S(2)}, u32[]{:S(2)}) async-start(bf16[16,2,2048]{2,1,0:T(2,128)(2,1)} %stack.7), calls=%async_computation | async-start | bytes 262144 | tf_op jit(solution)/shard_map/while/body/eval_jaxpr/all_to_all | solution.py:75
  497.2 7.7 collective-permute-start
  506.4 12.1 %all-to-all-start = ((bf16[16,2,2048]{2,1,0:T(2,128)(2,1)}), bf16[16,2,2048]{2,1,0:T(2,128)(2,1)S(1)}, u32[]{:S(2)}, u32[]{:S(2)}) async-start(bf16[16,2,2048]{2,1,0:T(2,128)(2,1)} %stack.7), calls=%async_computation | async-start | bytes 262144 | tf_op jit(solution)/shard_map/while/body/eval_jaxpr/all_to_all | solution.py:75
  527.7 12.1 %all-to-all-start = ((bf16[16,2,2048]{2,1,0:T(2,128)(2,1)}), bf16[16,2,2048]{2,1,0:T(2,128)(2,1)S(1)}, u32[]{:S(2)}, u32[]{:S(2)}) async-start(bf16[16,2,2048]{2,1,0:T(2,128)(2,1)} %stack.7), calls=%async_computation | async-start | bytes 262144 | tf_op jit(solution)/shard_map/while/body/eval_jaxpr/all_to_all | solution.py:75
  539.9 7.7 collective-permute-start
  549.1 12.1 %all-to-all-start = ((bf16[16,2,2048]{2,1,0:T(2,128)(2,1)}), bf16[16,2,2048]{2,1,0:T(2,128)(2,1)S(1)}, u32[]{:S(2)}, u32[]{:S(2)}) async-start(bf16[16,2,2048]{2,1,0:T(2,128)(2,1)} %stack.7), calls=%async_computation | async-start | bytes 262144 | tf_op jit(solution)/shard_map/while/body/eval_jaxpr/all_to_all | solution.py:75
  570.4 12.1 %all-to-all-start = ((bf16[16,2,2048]{2,1,0:T(2,128)(2,1)}), bf16[16,2,2048]{2,1,0:T(2,128)(2,1)S(1)}, u32[]{:S(2)}, u32[]{:S(2)}) async-start(bf16[16,2,2048]{2,1,0:T(2,128)(2,1)} %stack.7), calls=%async_computation | async-start | bytes 262144 | tf_op jit(solution)/shard_map/while/body/eval_jaxpr/all_to_all | solution.py:75
  591.7 12.1 %all-to-all-start = ((bf16[16,2,2048]{2,1,0:T(2,128)(2,1)}), bf16[16,2,2048]{2,1,0:T(2,128)(2,1)S(1)}, u32[]{:S(2)}, u32[]{:S(2)}) async-start(bf16[16,2,2048]{2,1,0:T(2,128)(2,1)} %stack.7), calls=%async_computation | async-start | bytes 262144 | tf_op jit(solution)/shard_map/while/body/eval_jaxpr/all_to_all | solution.py:75
  613.0 12.1 %all-to-all-start = ((bf16[16,2,2048]{2,1,0:T(2,128)(2,1)}), bf16[16,2,2048]{2,1,0:T(2,128)(2,1)S(1)}, u32[]{:S(2)}, u32[]{:S(2)}) async-start(bf16[16,2,2048]{2,1,0:T(2,128)(2,1)} %stack.7), calls=%async_computation | async-start | bytes 262144 | tf_op jit(solution)/shard_map/while/body/eval_jaxpr/all_to_all | solution.py:75
  634.3 12.1 %all-to-all-start = ((bf16[16,2,2048]{2,1,0:T(2,128)(2,1)}), bf16[16,2,2048]{2,1,0:T(2,128)(2,1)S(1)}, u32[]{:S(2)}, u32[]{:S(2)}) async-start(bf16[16,2,2048]{2,1,0:T(2,128)(2,1)} %stack.7), calls=%async_computation | async-start | bytes 262144 | tf_op jit(solution)/shard_map/while/body/eval_jaxpr/all_to_all | solution.py:75
  646.5 119.7 %collective-permute-start = (bf16[2,2048]{1,0:T(2,128)(2,1)S(1)}, bf16[2,2048]{1,0:T(2,128)(2,1)S(1)}, u32[]{:S(2)}, u32[]{:S(2)}) collective-permute-start(bf16[2,2048]{1,0:T(2,128)(2,1)S(1)} %get-tuple-element.355), channel_id=1, source_target_pairs={{0,16},{16,32},{32,48},{48,64},{64,80},{80,96},{96,112},{112,128},... | collective-permute-start | bytes 24584 | tf_op jit(solution)/shard_map/while/body/eval_jaxpr/ppermute | solution.py:14
  767.7 12.1 %all-to-all-start = ((bf16[16,2,2048]{2,1,0:T(2,128)(2,1)}), bf16[16,2,2048]{2,1,0:T(2,128)(2,1)S(1)}, u32[]{:S(2)}, u32[]{:S(2)}) async-start(bf16[16,2,2048]{2,1,0:T(2,128)(2,1)} %stack.7), calls=%async_computation | async-start | bytes 262144 | tf_op jit(solution)/shard_map/while/body/eval_jaxpr/all_to_all | solution.py:75
  786.2 8.9 %collective-permute-start = (bf16[2,2048]{1,0:T(2,128)(2,1)S(1)}, bf16[2,2048]{1,0:T(2,128)(2,1)S(1)}, u32[]{:S(2)}, u32[]{:S(2)}) collective-permute-start(bf16[2,2048]{1,0:T(2,128)(2,1)S(1)} %get-tuple-element.355), channel_id=1, source_target_pairs={{0,16},{16,32},{32,48},{48,64},{64,80},{80,96},{96,112},{112,128},... | collective-permute-start | bytes 24584 | tf_op jit(solution)/shard_map/while/body/eval_jaxpr/ppermute | solution.py:14
  796.6 12.1 %all-to-all-start = ((bf16[16,2,2048]{2,1,0:T(2,128)(2,1)}), bf16[16,2,2048]{2,1,0:T(2,128)(2,1)S(1)}, u32[]{:S(2)}, u32[]{:S(2)}) async-start(bf16[16,2,2048]{2,1,0:T(2,128)(2,1)} %stack.7), calls=%async_computation | async-start | bytes 262144 | tf_op jit(solution)/shard_map/while/body/eval_jaxpr/all_to_all | solution.py:75
  815.1 8.9 %collective-permute-start = (bf16[2,2048]{1,0:T(2,128)(2,1)S(1)}, bf16[2,2048]{1,0:T(2,128)(2,1)S(1)}, u32[]{:S(2)}, u32[]{:S(2)}) collective-permute-start(bf16[2,2048]{1,0:T(2,128)(2,1)S(1)} %get-tuple-element.355), channel_id=1, source_target_pairs={{0,16},{16,32},{32,48},{48,64},{64,80},{80,96},{96,112},{112,128},... | collective-permute-start | bytes 24584 | tf_op jit(solution)/shard_map/while/body/eval_jaxpr/ppermute | solution.py:14
  825.5 12.1 %all-to-all-start = ((bf16[16,2,2048]{2,1,0:T(2,128)(2,1)}), bf16[16,2,2048]{2,1,0:T(2,128)(2,1)S(1)}, u32[]{:S(2)}, u32[]{:S(2)}) async-start(bf16[16,2,2048]{2,1,0:T(2,128)(2,1)} %stack.7), calls=%async_computation | async-start | bytes 262144 | tf_op jit(solution)/shard_map/while/body/eval_jaxpr/all_to_all | solution.py:75
  (24 other events, 159.7 us)
